TPU v7x, 256 devices: a whole 4x4x8 slice. The times are simulated.
256 devices in a mesh: orient: 16 (over y, x_lo, core), strip: 16 (over x_hi, z).
Axes of the slice: x: 4 (x_hi: 2, x_lo: 2; x = x_hi * 2 + x_lo), y: 4, z: 8, core: 2. Of those that a mesh axis runs over, the one named last changes fastest.
Arguments:
- inflow_field: bfloat16 [32, 8, 128, 512], P('orient', None, 'strip'), may hold values from -6 to 6
- kernel_one: bfloat16 [32, 9, 8, 8], replicated, may hold values from -0.125 to 0.125
- kernel_two: bfloat16 [32, 9, 8, 8], replicated, may hold values from -0.125 to 0.125
- turbine_mask: int32 [128, 512], P('strip'), may hold values 0 or 1
- wind_sector: int32 [1], replicated, may hold values from 0 to 31
- wake_cotangent: bfloat16 [32, 8, 128, 512], P('orient', None, 'strip'), may hold values from -6 to 6
Outputs:
- wake_out: bfloat16 [32, 8, 128, 512], P('orient', None, 'strip')
- kernel_grad_one: float32 [32, 9, 8, 8], replicated
- kernel_grad_two: float32 [32, 9, 8, 8], replicated
Inputs may be any that keep to these rules, and one draw needn't show every extreme that they name: `wind_sector`: names one element of the group.
All inputs are finite; a program needn't handle non-finite values. No bound on the sum of `turbine_mask` on one device may be relied on, other than what follows from the above.
Results may differ from a plain program's by a relative error of at most 0.0051.
Values may be sent and summed in bfloat16 or wider, within the bound.
No kernel may reach another device: no remote copies, remote signals or barrier semaphores. Data moves between devices by JAX's collectives and lax.ppermute only.
A program may use at most 128 MiB of HBM per device.

v0:
```python
import math

import jax
import jax.numpy as jnp
from jax import lax
from jax.sharding import PartitionSpec as P

G = 32


OFFSETS = ((0, 0), (0, 1), (0, 2), (1, 0), (1, 1), (1, 2), (2, 0), (2, 1), (2, 2))


def with_halo(shard, sides, width):
    for axis, dim in sides:
        count, length = (lax.axis_size(axis), shard.shape[dim])
        up = [(i, (i + 1) % count) for i in range(count - 1)]
        down = [(j, i) for i, j in up]
        last = lax.slice_in_dim(shard, length - width, length, axis=dim)
        first = lax.slice_in_dim(shard, 0, width, axis=dim)
        before = lax.ppermute(last, axis, up)
        after = lax.ppermute(first, axis, down)
        shard = jnp.concatenate([before, shard, after], axis=dim)
    return shard


def relative(row_ids, col_ids, sector):
    halfway = G // 2
    row_rot = row_ids % halfway
    row_ref = row_ids // halfway
    col_rot = col_ids % halfway
    col_ref = col_ids // halfway
    sec_rot = sector % halfway
    sec_ref = sector // halfway
    moved_rot = (sec_rot + (1 - 2 * sec_ref) * col_rot) % halfway
    moved_ref = (sec_ref + col_ref) % 2
    inverse_rot = jnp.where(row_ref == 0, (halfway - row_rot) % halfway, row_rot)
    result_rot = (inverse_rot + (1 - 2 * row_ref) * moved_rot) % halfway
    result_ref = (row_ref + moved_ref) % 2
    return result_ref * halfway + result_rot


def kernel_block(kernel, row_ids, col_ids, sector):
    channels = kernel.shape[2]
    tap_count = kernel.shape[1]
    relation = relative(row_ids[:, None], col_ids[None, :], sector).reshape(-1)
    onehot = (relation[:, None] == jnp.arange(G, dtype=jnp.int32)[None, :]).astype(jnp.bfloat16)
    picked = jnp.dot(onehot, kernel.reshape(G, -1), preferred_element_type=jnp.float32)
    picked = picked.reshape(row_ids.shape[0], col_ids.shape[0], tap_count, channels, channels)
    picked = picked.transpose(2, 0, 3, 1, 4)
    return picked.reshape(
        tap_count, row_ids.shape[0] * channels, col_ids.shape[0] * channels
    ).astype(jnp.bfloat16)


def fold_kernel(partial_grad, row_ids, col_ids, sector):
    tap_count = partial_grad.shape[0]
    channels = partial_grad.shape[1] // row_ids.shape[0]
    relation = relative(row_ids[:, None], col_ids[None, :], sector).reshape(-1)
    onehot = (relation[:, None] == jnp.arange(G, dtype=jnp.int32)[None, :]).astype(jnp.float32)
    arranged = partial_grad.reshape(
        tap_count, row_ids.shape[0], channels, col_ids.shape[0], channels
    )
    arranged = arranged.transpose(1, 3, 0, 2, 4).reshape(relation.shape[0], -1)
    folded = jnp.dot(
        onehot.T, arranged, precision=lax.Precision.HIGHEST, preferred_element_type=jnp.float32
    )
    return folded.reshape(G, tap_count, channels, channels)


def place_forward(mixed_taps, height, extent):
    padded = jnp.pad(mixed_taps, ((0, 0), (0, 0), (0, 0), (1, 1)))
    summed = jnp.zeros((mixed_taps.shape[1], height, extent), jnp.float32)
    for tap_index, (row_shift, col_shift) in enumerate(OFFSETS):
        summed = (
            summed
            + padded[tap_index, :, row_shift : row_shift + height, col_shift : col_shift + extent]
        )
    return summed


def place_backward(mixed_taps, height, extent):
    padded = jnp.pad(mixed_taps, ((0, 0), (0, 0), (0, 0), (1, 1)))
    summed = jnp.zeros((mixed_taps.shape[1], height, extent), jnp.float32)
    for tap_index, (row_shift, col_shift) in enumerate(OFFSETS):
        summed = (
            summed
            + padded[
                tap_index,
                :,
                2 - row_shift : 2 - row_shift + height,
                2 - col_shift : 2 - col_shift + extent,
            ]
        )
    return summed


def layer_forward(source, weights_row):
    tap_count, local_width, full_width = weights_row.shape
    height, extent = (source.shape[1], source.shape[2])
    matrix = weights_row.reshape(tap_count * local_width, full_width)
    widened = with_halo(source, (("strip", 1),), 1)
    gathered = lax.all_gather(widened, "orient", axis=0, tiled=True)
    mixed_taps = jnp.dot(
        matrix, gathered.reshape(full_width, -1), preferred_element_type=jnp.float32
    )
    mixed_taps = mixed_taps.reshape(tap_count, local_width, gathered.shape[1], extent)
    center = gathered[:, 1 : height + 1]
    return (place_forward(mixed_taps, height, extent), center)


def rim_rows(gradient):
    return with_halo(gradient, (("strip", 1),), 1)


def weight_grad(cot_rows, center):
    height, extent = (center.shape[1], center.shape[2])
    padded = jnp.pad(cot_rows, ((0, 0), (0, 0), (1, 1)))
    flat_center = center.reshape(center.shape[0], -1)
    pieces = []
    for row_shift, col_shift in OFFSETS:
        window = padded[
            :, 2 - row_shift : 2 - row_shift + height, 2 - col_shift : 2 - col_shift + extent
        ]
        window = window.reshape(cot_rows.shape[0], -1)
        pieces.append(
            lax.dot_general(
                window, flat_center, (((1,), (1,)), ((), ())), preferred_element_type=jnp.float32
            )
        )
    return jnp.stack(pieces, 0)


def shards(inflow_field, kernel_one, kernel_two, turbine_mask, wind_sector, wake_cotangent):
    groups, channels, height, extent = inflow_field.shape
    local_width = groups * channels
    sector = wind_sector[0]
    neutral = jnp.int32(0)
    all_groups = jnp.arange(G, dtype=jnp.int32)
    scale_factor = 1.0 / math.sqrt(G * height * lax.axis_size("strip") * extent)
    first_group = lax.axis_index("orient") * groups
    my_groups = first_group + jnp.arange(groups, dtype=jnp.int32)
    row_one = kernel_block(kernel_one, my_groups, all_groups, sector)
    row_two = kernel_block(kernel_two, my_groups, all_groups, neutral)
    open_cells = (1 - turbine_mask).astype(jnp.float32)
    source = inflow_field.reshape(local_width, height, extent)
    first_pre, first_center = layer_forward(source, row_one)
    sigmoid_one = jax.nn.sigmoid(first_pre)
    hidden = (first_pre * sigmoid_one * open_cells).astype(jnp.bfloat16)
    second_pre, second_center = layer_forward(hidden, row_two)
    wake_out = second_pre.astype(jnp.bfloat16).reshape(groups, channels, height, extent)
    cotangent = wake_cotangent.reshape(local_width, height, extent)
    cot_two = rim_rows(cotangent)
    grad_two = weight_grad(cot_two, second_center)
    rows_turned = row_two.transpose(0, 2, 1)
    mixed_taps = jnp.dot(
        rows_turned.reshape(9 * (local_width * lax.axis_size("orient")), local_width),
        cot_two.reshape(local_width, -1),
        preferred_element_type=jnp.float32,
    )
    mixed_taps = mixed_taps.reshape(9, local_width * lax.axis_size("orient"), height + 2, extent)
    back_grad = lax.psum_scatter(
        place_backward(mixed_taps, height, extent), "orient", scatter_dimension=0, tiled=True
    )
    first_grad = (
        back_grad * open_cells * sigmoid_one * (1.0 + first_pre * (1.0 - sigmoid_one))
    ).astype(jnp.bfloat16)
    cot_one = rim_rows(first_grad)
    grad_one = weight_grad(cot_one, first_center)
    share_one = fold_kernel(grad_one, my_groups, all_groups, sector) * scale_factor
    share_two = fold_kernel(grad_two, my_groups, all_groups, neutral) * scale_factor
    summed_one, summed_two = lax.psum((share_one, share_two), ("orient", "strip"))
    return (wake_out, summed_one, summed_two)


def solution(mesh):
    return jax.shard_map(
        shards,
        mesh=mesh,
        in_specs=(
            P("orient", None, "strip", None),
            P(),
            P(),
            P("strip", None),
            P(),
            P("orient", None, "strip", None),
        ),
        out_specs=(P("orient", None, "strip", None), P(), P()),
        check_vma=False,
    )
```

profile of v0, /device:TPU:1, one launch (start us, length us, event | category | flops | bytes accessed | tf_op | source)
XLA Modules:
  0.0 479.3 jit_solution(5787390711143419611)
XLA Ops:
  7.2 0.9 copy.98
  8.2 4.4 collective-permute-start
  12.5 1.3 collective-permute-start.1
  13.8 3.4 collective-permute-done.1
  17.2 0.7 pad_maximum_fusion
  18.0 0.9 copy.97
  18.9 3.5 collective-permute-start.4
  22.5 1.3 collective-permute-start.5
  24.6 1.3 fusion.13
  25.9 0.7 copy.32
  26.7 1.8 convert_element_type.51
  28.5 18.8 %fusion.60 = f32[9,256,10,512]{3,1,2,0:T(8,128)} fusion(bf16[9,16,256]{2,1,0:T(8,128)(2,1)S(1)} %convert_element_type.51, bf16[10,2,8,512]{3,2,1,0:T(8,128)(2,1)S(1)} %get-tuple-element.21), kind=kOutput, calls=%fused_computation.112 | convolution fusion | flops 377487360 | bytes 47423488 | tf_op jit(solution)/shard_map/dot_general | solution.py:156
  47.3 17.4 %fusion.8 = f32[256,8,512]{2,0,1:T(8,128)} fusion(f32[9,256,10,512]{3,1,2,0:T(8,128)} %fusion.60), kind=kLoop, calls=%fused_computation.26 | loop fusion | flops 8388608 | bytes 63963136 | tf_op jit(solution)/shard_map/add | solution.py:87
  66.0 0.7 copy.34
  66.8 1.7 reshape.552
  68.6 4.4 copy.36
  73.0 2.7 fusion.11
  75.7 65.7 %reduce-scatter.2.cloned.1.call-done = f32[16,8,512]{2,0,1:T(8,128)} async-done(((f32[256,8,512]{2,0,1:T(8,128)}), f32[16,8,512]{2,0,1:T(8,128)}) %reduce-scatter.2.cloned.1.call-update) | async-done | bytes 262160 | tf_op jit(solution)/shard_map/reduce_scatter | solution.py:162
  141.4 1.4 fusion.49
  143.0 3.0 collective-permute-start.2
  145.9 1.3 collective-permute-start.3
  147.3 3.3 collective-permute-done.3
  150.5 0.7 pad_maximum_fusion.1
  151.3 3.4 reshape.554
  156.2 3.6 collective-permute-start.6
  159.8 1.3 collective-permute-start.7
  161.1 2.2 convolution_bitcast_fusion.14
  165.7 0.9 fusion.59
  168.2 1.6 convolution_bitcast_fusion.16
  170.0 1.6 convolution_bitcast_fusion.15
  171.8 0.7 copy.44
  172.5 1.5 convolution_bitcast_fusion.13
  174.3 0.7 copy.46
  175.0 1.6 convolution_bitcast_fusion.12
  176.8 0.8 copy.47
  177.5 1.6 convolution_bitcast_fusion.11
  180.4 1.3 convolution_multiply_fusion.1
  181.7 10.1 %all-gather.5.cloned.1.call-done = bf16[256,10,512]{2,0,1:T(8,128)(2,1)} async-done(((bf16[16,10,512]{2,0,1:T(8,128)(2,1)}), bf16[256,10,512]{2,0,1:T(8,128)(2,1)}) %all-gather.5.cloned.1.call-update) | async-done | bytes 2621456 | tf_op jit(solution)/shard_map/all_gather | solution.py:103
  191.8 2.4 convolution_bitcast_fusion.10
  200.8 0.8 copy.58
  208.5 1.5 copy.61
  210.3 1.3 convolution_multiply_fusion
  211.7 2.6 copy.37
  214.3 2.7 fusion.9
  217.5 0.7 copy.63
  218.3 250.8 %all-reduce.8.cloned.1.call-done = (f32[32,9,8,8]{0,1,3,2:T(8,128)}, f32[32,9,8,8]{0,1,3,2:T(8,128)}) async-done(((f32[32,9,8,8]{0,1,3,2:T(8,128)}, f32[32,9,8,8]{0,1,3,2:T(8,128)}), (f32[32,9,8,8]{0,1,3,2:T(8,128)}, f32[32,9,8,8]{0,1,3,2:T(8,128)})) %all-reduce.8.cloned.1.call-update) | async-done | bytes 147472 | tf_op jit(solution)/shard_map/psum | solution.py:172
  469.0 1.9 copy.64
  470.9 1.9 copy.65
  (129 shorter events, 23.4 us)
Async XLA Ops:
  7.2 61.4 %all-gather.3.cloned.1.call-start = ((), (), s32[]{:S(2)}) async-start(), calls=%async_computation.1 | async-start | bytes 2785280 | tf_op jit(solution)/shard_map/all_gather | solution.py:103
  8.2 5.7 %collective-permute-start = (bf16[16,1,512]{2,0,1:T(8,128)(2,1)S(1)}, bf16[16,1,512]{2,0,1:T(8,128)(2,1)S(1)}, u32[]{:S(2)}, u32[]{:S(2)}) collective-permute-start(bf16[16,1,512]{2,0,1:T(8,128)(2,1)S(1)} %get-tuple-element.26), channel_id=1, source_target_pairs={{0,1},{1,2},{2,3},{3,4},{4,5},{5,6},{6,7},{7,8},{8,9},{9,10},{10,1... | collective-permute-start | bytes 49160 | tf_op jit(solution)/shard_map/ppermute | solution.py:21
  12.5 4.7 collective-permute-start.1
  17.9 123.5 %reduce-scatter.2.cloned.1.call-start = ((), (), s32[]{:S(2)}) async-start(), calls=%async_computation.3 | async-start | bytes 4456448 | tf_op jit(solution)/shard_map/reduce_scatter | solution.py:162
  18.9 9.5 %collective-permute-start.4 = (bf16[16,1,512]{2,0,1:T(8,128)(2,1)S(1)}, bf16[16,1,512]{2,0,1:T(8,128)(2,1)S(1)}, u32[]{:S(2)}, u32[]{:S(2)}) collective-permute-start(bf16[16,1,512]{2,0,1:T(8,128)(2,1)S(1)} %get-tuple-element.28), channel_id=1, source_target_pairs={{0,1},{1,2},{2,3},{3,4},{4,5},{5,6},{6,7},{7,8},{8,9},{9,10},{10,1... | collective-permute-start | bytes 49160 | tf_op jit(solution)/shard_map/ppermute | solution.py:21
  22.5 6.0 %collective-permute-start.5 = (bf16[16,1,512]{2,0,1:T(8,128)(2,1)S(1)}, bf16[16,1,512]{2,0,1:T(8,128)(2,1)S(1)}, u32[]{:S(2)}, u32[]{:S(2)}) collective-permute-start(bf16[16,1,512]{2,0,1:T(8,128)(2,1)S(1)} %get-tuple-element.29), channel_id=1, source_target_pairs={{1,0},{2,1},{3,2},{4,3},{5,4},{6,5},{7,6},{8,7},{9,8},{10,9},{11,1... | collective-permute-start | bytes 49160 | tf_op jit(solution)/shard_map/ppermute | solution.py:22
  26.7 20.6 %copy-start.1 = (bf16[9,2,8,32,8]{4,3,2,1,0:T(8,128)(2,1)}, bf16[9,2,8,32,8]{4,3,2,1,0:T(8,128)(2,1)S(1)}, u32[]{:S(2)}) copy-start(bf16[9,2,8,32,8]{4,3,2,1,0:T(8,128)(2,1)S(1)} %copy.32) | copy-start | bytes 221188
  64.7 0.9 copy-start.4
  64.7 3.8 copy-start.12
  64.7 127.1 %all-gather.5.cloned.1.call-start = ((), (), s32[]{:S(2)}) async-start(), calls=%async_computation.2 | async-start | bytes 2785280 | tf_op jit(solution)/shard_map/all_gather | solution.py:103
  142.9 20.8 %copy-start.2 = (bf16[256,10,512]{2,0,1:T(8,128)(2,1)S(1)}, bf16[256,10,512]{2,0,1:T(8,128)(2,1)}, u32[]{:S(2)}) copy-start(bf16[256,10,512]{2,0,1:T(8,128)(2,1)} %all-gather.3.cloned.1.call-done) | copy-start | bytes 7864324
  143.0 4.3 collective-permute-start.2
  145.9 4.6 collective-permute-start.3
  151.2 317.8 %all-reduce.8.cloned.1.call-start = ((), (), s32[]{:S(2)}) async-start(), calls=%async_computation.4 | async-start | bytes 2097152 | tf_op jit(solution)/shard_map/psum | solution.py:172
  156.2 7.5 %collective-permute-start.6 = (bf16[16,1,512]{2,0,1:T(8,128)(2,1)S(1)}, bf16[16,1,512]{2,0,1:T(8,128)(2,1)S(1)}, u32[]{:S(2)}, u32[]{:S(2)}) collective-permute-start(bf16[16,1,512]{2,0,1:T(8,128)(2,1)S(1)} %get-tuple-element.22), channel_id=1, source_target_pairs={{0,1},{1,2},{2,3},{3,4},{4,5},{5,6},{6,7},{7,8},{8,9},{9,10},{10,1... | collective-permute-start | bytes 49160 | tf_op jit(solution)/shard_map/ppermute | solution.py:21
  159.8 4.9 %collective-permute-start.7 = (bf16[16,1,512]{2,0,1:T(8,128)(2,1)S(1)}, bf16[16,1,512]{2,0,1:T(8,128)(2,1)S(1)}, u32[]{:S(2)}, u32[]{:S(2)}) collective-permute-start(bf16[16,1,512]{2,0,1:T(8,128)(2,1)S(1)} %get-tuple-element.23), channel_id=1, source_target_pairs={{1,0},{2,1},{3,2},{4,3},{5,4},{6,5},{7,6},{8,7},{9,8},{10,9},{11,1... | collective-permute-start | bytes 49160 | tf_op jit(solution)/shard_map/ppermute | solution.py:22
  164.7 0.6 copy-start.11
  166.5 0.7 copy-start.10
  177.5 1.9 copy-start.8
  177.5 2.0 copy-start.7
  177.5 2.0 copy-start.9
  177.5 2.9 copy-start.14
  191.8 3.3 copy-start
  196.1 1.9 copy-start.3
  202.2 4.4 copy-start.6
  202.5 7.8 %copy-start.13 = (s32[64]{0:T(128)S(1)}, s32[64]{0:T(128)}, u32[]{:S(2)}) copy-start(s32[64]{0:T(128)} %fusion.114) | copy-start | bytes 772
  211.7 2.6 copy-start.5
Sparse Core Ops, SparseCore 0:
  18.0 41.6 all-gather.2
  64.8 76.5 reduce-scatter.1
  151.3 40.4 all-gather.4
  211.8 257.2 all-reduce.7
where the time goes:
time: 481 us; the launch traced here: 479 us
  waiting for transfers between devices  333 us (69%)
  matrix products  48.1 us (10%)
  local copies, waits for them, and re-layouts  39.6 us (8%)
  other arithmetic  23 us (5%)
  starting transfers between devices  20 us (4%)
  between operations  15 us (3%)
    psum x1, waiting for transfers between devices, shards(): lax.psum((share_one, share_two), ('orient', 'strip'))  251 us
    reduce_scatter x1, waiting for transfers between devices, shards(): lax.psum_scatter(place_backward(mixed_taps, height, extent), 'orient', sc...  65.7 us
    dot_general x18, matrix products, weight_grad(): lax.dot_general(window, flat_center, (((1,), (1,)), ((), ())), preferred_...  19.6 us
    dot_general x1, matrix products, shards(): jnp.dot(rows_turned.reshape(9 * (local_width * lax.axis_size('orient')),...  18.8 us
    add x1, other arithmetic, place_backward(): summed + padded[tap_index, :, 2 - row_shift:2 - row_shift + height, 2 - c...  17.4 us
    ppermute x4, starting transfers between devices, with_halo(): before = lax.ppermute(last, axis, up)  14.5 us
    unnamed x51, local copies, waits for them, and re-layouts  12.8 us
    all_gather x2, waiting for transfers between devices, layer_forward(): gathered = lax.all_gather(widened, 'orient', axis=0, tiled=True)  10.1 us
  transfers between devices with their start and end apart: 12, of which 6 were waited for; matrix products, arithmetic and copies ran while one was open for 17% of the time, Pallas kernels for 0%

commit v1 on v0

--- a/solution.py
+++ b/solution.py
@@ -129,6 +129,13 @@
             )
         )
     return jnp.stack(pieces, 0)
+
+
+def all_sum(flat, axes):
+    count = lax.axis_size(axes)
+    parts = lax.all_to_all(flat.reshape(count, -1), axes, 0, 0, tiled=True).sum(0)
+    spread = jnp.broadcast_to(parts[None], (count,) + parts.shape)
+    return lax.all_to_all(spread, axes, 0, 0, tiled=True).reshape(-1)
 
 
 def shards(inflow_field, kernel_one, kernel_two, turbine_mask, wind_sector, wake_cotangent):
@@ -152,16 +159,16 @@
     cotangent = wake_cotangent.reshape(local_width, height, extent)
     cot_two = rim_rows(cotangent)
     grad_two = weight_grad(cot_two, second_center)
-    rows_turned = row_two.transpose(0, 2, 1)
+    cot_all = lax.all_gather(cot_two, "orient", axis=0, tiled=True)
+    col_two = kernel_block(kernel_two, all_groups, my_groups, neutral)
+    cols_turned = col_two.transpose(0, 2, 1)
     mixed_taps = jnp.dot(
-        rows_turned.reshape(9 * (local_width * lax.axis_size("orient")), local_width),
-        cot_two.reshape(local_width, -1),
+        cols_turned.reshape(9 * local_width, local_width * lax.axis_size("orient")),
+        cot_all.reshape(local_width * lax.axis_size("orient"), -1),
         preferred_element_type=jnp.float32,
     )
-    mixed_taps = mixed_taps.reshape(9, local_width * lax.axis_size("orient"), height + 2, extent)
-    back_grad = lax.psum_scatter(
-        place_backward(mixed_taps, height, extent), "orient", scatter_dimension=0, tiled=True
-    )
+    mixed_taps = mixed_taps.reshape(9, local_width, height + 2, extent)
+    back_grad = place_backward(mixed_taps, height, extent)
     first_grad = (
         back_grad * open_cells * sigmoid_one * (1.0 + first_pre * (1.0 - sigmoid_one))
     ).astype(jnp.bfloat16)
@@ -169,7 +176,11 @@
     grad_one = weight_grad(cot_one, first_center)
     share_one = fold_kernel(grad_one, my_groups, all_groups, sector) * scale_factor
     share_two = fold_kernel(grad_two, my_groups, all_groups, neutral) * scale_factor
-    summed_one, summed_two = lax.psum((share_one, share_two), ("orient", "strip"))
+    flat = jnp.concatenate([share_one.reshape(-1), share_two.reshape(-1)])
+    flat = all_sum(flat, ("orient", "strip"))
+    summed_one, summed_two = jnp.split(flat, 2)
+    summed_one = summed_one.reshape(share_one.shape)
+    summed_two = summed_two.reshape(share_two.shape)
     return (wake_out, summed_one, summed_two)
 
 

time: 481 us -> 247 us (0.51)
  waiting for transfers between devices: 333 us -> 97.5 us
  starting transfers between devices: 20 us -> 37.7 us
  local copies, waits for them, and re-layouts: 39.6 us -> 57.2 us
  other arithmetic: 23 us -> 6.11 us
  matrix products: 48.1 us -> 31.7 us
    psum x1 -> x0, waiting for transfers between devices: 251 us -> none  [shards(): lax.psum((share_one, share_two), ('orient', 'strip'))]
    reduce_scatter x1 -> x0, waiting for transfers between devices: 65.7 us -> none  [shards(): lax.psum_scatter(place_backward(mixed_taps, height, extent), 'orient', sc...]
    all_gather x0 -> x1, waiting for transfers between devices: none -> 32.5 us  [shards(): cot_all = lax.all_gather(cot_two, 'orient', axis=0, tiled=True)]
    all_gather x2, waiting for transfers between devices: 10.1 us -> 33.7 us  [layer_forward(): gathered = lax.all_gather(widened, 'orient', axis=0, tiled=True)]
    all_to_all x0 -> x2, waiting for transfers between devices: none -> 19.4 us  [the longest x1 11.7 us: all_sum(): return lax.all_to_all(spread, axes, 0, 0, tiled=True).reshape(-1)]
    all_to_all x0 -> x2, starting transfers between devices: none -> 17.7 us  [the longest x1 11.7 us: all_sum(): lax.all_to_all(flat.reshape(count, -1), axes, 0, 0, tiled=True).sum(0)]
    add x1 -> x0, other arithmetic: 17.4 us -> none  [place_backward(): summed + padded[tap_index, :, 2 - row_shift:2 - row_shift + height, 2 - c...]
    dot_general x1, matrix products: 18.8 us -> 2.74 us  [shards(): jnp.dot(cols_turned.reshape(9 * local_width, local_width * lax.axis_size(...]
  transfers between devices with their start and end apart: 12 -> 13, of which waited for: 6 -> 9; matrix products, arithmetic and copies ran while one was open for 17% -> 20% of each run, Pallas kernels for 0% -> 0%
where the time goes in v1:
time: 247 us; the launch traced here: 245 us
  waiting for transfers between devices  97.5 us (39%)
  local copies, waits for them, and re-layouts  57.2 us (23%)
  starting transfers between devices  37.7 us (15%)
  matrix products  31.7 us (13%)
  between operations  15.1 us (6%)
  other arithmetic  6.11 us (2%)
    all_gather x2, waiting for transfers between devices, layer_forward(): gathered = lax.all_gather(widened, 'orient', axis=0, tiled=True)  33.7 us
    all_gather x1, waiting for transfers between devices, shards(): cot_all = lax.all_gather(cot_two, 'orient', axis=0, tiled=True)  32.5 us
    dot_general x18, matrix products, weight_grad(): lax.dot_general(window, flat_center, (((1,), (1,)), ((), ())), preferred_...  19.5 us
    ppermute x4, starting transfers between devices, with_halo(): before = lax.ppermute(last, axis, up)  14.5 us
    ppermute x4, waiting for transfers between devices, with_halo(): after = lax.ppermute(first, axis, down)  11.9 us
    all_to_all x1, waiting for transfers between devices, all_sum(): return lax.all_to_all(spread, axes, 0, 0, tiled=True).reshape(-1)  11.7 us
    all_to_all x1, starting transfers between devices, all_sum(): lax.all_to_all(flat.reshape(count, -1), axes, 0, 0, tiled=True).sum(0)  11.7 us
    unnamed x48, local copies, waits for them, and re-layouts  11.5 us
  transfers between devices with their start and end apart: 13, of which 9 were waited for; matrix products, arithmetic and copies ran while one was open for 20% of the time, Pallas kernels for 0%

profile of v1, /device:TPU:1, one launch (start us, length us, event | category | flops | bytes accessed | tf_op | source)
XLA Modules:
  0.0 245.4 jit_solution(18177947647932420527)
XLA Ops:
  7.2 0.9 copy.130
  8.2 4.5 %collective-permute-start = (bf16[16,1,512]{2,0,1:T(8,128)(2,1)S(1)}, bf16[16,1,512]{2,0,1:T(8,128)(2,1)S(1)}, u32[]{:S(2)}, u32[]{:S(2)}) collective-permute-start(bf16[16,1,512]{2,0,1:T(8,128)(2,1)S(1)} %get-tuple-element.27), channel_id=1, source_target_pairs={{0,1},{1,2},{2,3},{3,4},{4,5},{5,6},{6,7},{7,8},{8,9},{9,10},{10,1... | collective-permute-start | bytes 49160 | tf_op jit(solution)/shard_map/ppermute | solution.py:21
  12.7 1.3 collective-permute-start.1
  14.0 3.4 %collective-permute-done.1 = bf16[16,1,512]{2,0,1:T(8,128)(2,1)S(1)} collective-permute-done((bf16[16,1,512]{2,0,1:T(8,128)(2,1)S(1)}, bf16[16,1,512]{2,0,1:T(8,128)(2,1)S(1)}, u32[]{:S(2)}, u32[]{:S(2)}) %collective-permute-start.1) | collective-permute-done | bytes 16416 | tf_op jit(solution)/shard_map/ppermute | solution.py:22
  18.1 0.9 copy.129
  19.1 3.5 %collective-permute-start.4 = (bf16[16,1,512]{2,0,1:T(8,128)(2,1)S(1)}, bf16[16,1,512]{2,0,1:T(8,128)(2,1)S(1)}, u32[]{:S(2)}, u32[]{:S(2)}) collective-permute-start(bf16[16,1,512]{2,0,1:T(8,128)(2,1)S(1)} %get-tuple-element.29), channel_id=1, source_target_pairs={{0,1},{1,2},{2,3},{3,4},{4,5},{5,6},{6,7},{7,8},{8,9},{9,10},{10,1... | collective-permute-start | bytes 49160 | tf_op jit(solution)/shard_map/ppermute | solution.py:21
  22.6 1.3 collective-permute-start.5
  23.9 4.6 %collective-permute-done.5 = bf16[16,1,512]{2,0,1:T(8,128)(2,1)S(1)} collective-permute-done((bf16[16,1,512]{2,0,1:T(8,128)(2,1)S(1)}, bf16[16,1,512]{2,0,1:T(8,128)(2,1)S(1)}, u32[]{:S(2)}, u32[]{:S(2)}) %collective-permute-start.5) | collective-permute-done | bytes 16416 | tf_op jit(solution)/shard_map/ppermute | solution.py:22
  30.7 1.3 fusion.10
  32.7 1.7 reshape.863
  35.8 1.7 convert_element_type.71
  37.6 22.3 %all-gather.4.cloned.1.call-done = bf16[256,10,512]{2,0,1:T(8,128)(2,1)} async-done(((bf16[16,10,512]{2,0,1:T(8,128)(2,1)}), bf16[256,10,512]{2,0,1:T(8,128)(2,1)}) %all-gather.4.cloned.1.call-update) | async-done | bytes 2621456 | tf_op jit(solution)/shard_map/all_gather | solution.py:103
  59.9 4.4 %copy.53 = bf16[256,10,512]{0,2,1:T(8,128)(2,1)} copy(bf16[256,10,512]{2,0,1:T(8,128)(2,1)} %all-gather.4.cloned.1.call-done) | data formatting | bytes 5242880 | tf_op jit(solution)/shard_map/all_gather | solution.py:103
  64.3 2.7 %fusion.4 = f32[9,16,10,512]{3,1,2,0:T(8,128)S(1)} fusion(bf16[256,10,512]{0,2,1:T(8,128)(2,1)} %copy.53, bf16[9,16,256,1]{2,1,0,3:T(8,128)(2,1)S(1)} %reshape.863), kind=kOutput, calls=%fused_computation.22 | convolution fusion | flops 377487360 | bytes 5644288 | tf_op jit(solution)/shard_map/dot_general | solution.py:104
  67.1 32.5 %all-gather.8.cloned.1.call-done = bf16[256,10,512]{2,0,1:T(8,128)(2,1)} async-done(((bf16[16,10,512]{2,0,1:T(8,128)(2,1)}), bf16[256,10,512]{2,0,1:T(8,128)(2,1)}) %all-gather.8.cloned.1.call-update) | async-done | bytes 2621456 | tf_op jit(solution)/shard_map/all_gather | solution.py:162
  99.6 4.4 %copy.58 = bf16[256,10,512]{0,2,1:T(8,128)(2,1)} copy(bf16[256,10,512]{2,0,1:T(8,128)(2,1)} %all-gather.8.cloned.1.call-done) | data formatting | bytes 5242880 | tf_op jit(solution)/shard_map/all_gather | solution.py:162
  104.0 2.7 %fusion = f32[9,16,10,512]{3,1,2,0:T(8,128)S(1)} fusion(bf16[256,10,512]{0,2,1:T(8,128)(2,1)} %copy.58, bf16[9,256,16]{1,2,0:T(8,128)(2,1)S(1)} %convert_element_type.71), kind=kOutput, calls=%fused_computation.18 | convolution fusion | flops 377487360 | bytes 5644288 | tf_op jit(solution)/shard_map/dot_general | solution.py:165
  106.8 1.6 fusion.93
  108.5 3.3 %collective-permute-start.2 = (bf16[16,1,512]{2,0,1:T(8,128)(2,1)S(1)}, bf16[16,1,512]{2,0,1:T(8,128)(2,1)S(1)}, u32[]{:S(2)}, u32[]{:S(2)}) collective-permute-start(bf16[16,1,512]{2,0,1:T(8,128)(2,1)S(1)} %get-tuple-element.25), channel_id=1, source_target_pairs={{0,1},{1,2},{2,3},{3,4},{4,5},{5,6},{6,7},{7,8},{8,9},{9,10},{10,1... | collective-permute-start | bytes 49160 | tf_op jit(solution)/shard_map/ppermute | solution.py:21
  111.8 1.3 collective-permute-start.3
  113.1 3.2 %collective-permute-done.3 = bf16[16,1,512]{2,0,1:T(8,128)(2,1)S(1)} collective-permute-done((bf16[16,1,512]{2,0,1:T(8,128)(2,1)S(1)}, bf16[16,1,512]{2,0,1:T(8,128)(2,1)S(1)}, u32[]{:S(2)}, u32[]{:S(2)}) %collective-permute-start.3) | collective-permute-done | bytes 16416 | tf_op jit(solution)/shard_map/ppermute | solution.py:22
  117.9 3.2 %collective-permute-start.6 = (bf16[16,1,512]{2,0,1:T(8,128)(2,1)S(1)}, bf16[16,1,512]{2,0,1:T(8,128)(2,1)S(1)}, u32[]{:S(2)}, u32[]{:S(2)}) collective-permute-start(bf16[16,1,512]{2,0,1:T(8,128)(2,1)S(1)} %get-tuple-element.23), channel_id=1, source_target_pairs={{0,1},{1,2},{2,3},{3,4},{4,5},{5,6},{6,7},{7,8},{8,9},{9,10},{10,1... | collective-permute-start | bytes 49160 | tf_op jit(solution)/shard_map/ppermute | solution.py:21
  121.1 1.5 collective-permute-start.7
  122.6 3.0 %slice_bitcast_fusion = bf16[32,8,8,512]{3,1,0,2:T(8,128)(2,1)} fusion(bf16[256,10,512]{2,0,1:T(8,128)(2,1)} %all-gather.4.cloned.1.call-done), kind=kLoop, calls=%fused_computation.156 | loop fusion | bytes 4194304 | tf_op jit(solution)/shard_map/dot_general | solution.py:127
  129.5 1.6 convolution_bitcast_fusion.14
  132.0 1.5 convolution_bitcast_fusion.13
  133.9 1.6 convolution_bitcast_fusion.12
  136.7 1.6 convolution_bitcast_fusion.11
  138.7 3.1 %fusion.15 = f32[9,2,8,32,8]{3,2,4,1,0:T(8,128)S(1)} fusion(f32[9,2,8,32,8]{3,2,4,1,0:T(8,128)S(1)} %constant_dynamic-update-slice_fusion.4, bf16[32,8,8,512]{3,1,0,2:T(8,128)(2,1)} %slice_bitcast_fusion, bf16[2,8,8,512,1]{3,1,0,2,4:T(8,128)(2,1)S(1)} %copy-done.11), kind=kOutput, calls=%fused_computation.36 | convolution fusion | flops 33554432 | bytes 2293760 | tf_op jit(solution)/shard_map/dot_general | solution.py:127
  143.6 1.0 concatenate.40
  144.7 11.3 %all-gather.6.cloned.1.call-done = bf16[256,10,512]{2,0,1:T(8,128)(2,1)} async-done(((bf16[16,10,512]{2,0,1:T(8,128)(2,1)}), bf16[256,10,512]{2,0,1:T(8,128)(2,1)}) %all-gather.6.cloned.1.call-update) | async-done | bytes 2621456 | tf_op jit(solution)/shard_map/all_gather | solution.py:103
  156.0 2.4 convolution_bitcast_fusion.10
  171.4 0.8 constant_dynamic-update-slice_fusion.14
  178.1 1.5 copy.81
  180.7 1.5 copy.83
  182.2 1.6 concatenate.43
  183.9 1.0 copy.84
  184.8 11.7 %all-to-all-start = ((f32[256,1,144]{2,1,0:T(1,128)}), f32[256,1,144]{2,1,0:T(1,128)S(1)}, u32[]{:S(2)}, u32[]{:S(2)}) async-start(f32[256,1,144]{2,1,0:T(1,128)} %copy.84), calls=%async_computation | async-start | bytes 524288 | tf_op jit(solution)/shard_map/all_to_all | solution.py:136
  196.5 1.1 fusion.9
  197.6 1.5 copy.49
  199.1 2.8 %reshape.865 = bf16[9,16,256,1]{2,1,0,3:T(8,128)(2,1)S(1)} reshape(bf16[9,2,8,32,8]{4,3,2,1,0:T(8,128)(2,1)} %copy.49) | data formatting | bytes 147456 | tf_op jit(solution)/shard_map/convert_element_type | solution.py:53
  201.8 2.6 %copy.54 = bf16[256,10,512]{0,2,1:T(8,128)(2,1)} copy(bf16[256,10,512]{2,0,1:T(8,128)(2,1)S(1)} %copy-done) | data formatting | bytes 5242880 | tf_op jit(solution)/shard_map/all_gather | solution.py:103
  204.5 7.7 %all-to-all-done = f32[256,1,144]{2,1,0:T(1,128)S(1)} async-done(((f32[256,1,144]{2,1,0:T(1,128)}), f32[256,1,144]{2,1,0:T(1,128)S(1)}, u32[]{:S(2)}, u32[]{:S(2)}) %all-to-all-start) | async-done | bytes 147488 | tf_op jit(solution)/shard_map/all_to_all | solution.py:136
  213.3 6.0 %all-to-all-start.1 = ((f32[256,1,144]{2,1,0:T(1,128)}), f32[256,1,144]{2,1,0:T(1,128)S(1)}, u32[]{:S(2)}, u32[]{:S(2)}) async-start(f32[256,1,144]{2,1,0:T(1,128)} %broadcast_in_dim.2), calls=%async_computation.1 | async-start | bytes 524288 | tf_op jit(solution)/shard_map/all_to_all | solution.py:138
  219.3 2.7 %fusion.2 = f32[9,16,10,512]{3,1,2,0:T(8,128)S(1)} fusion(bf16[256,10,512]{0,2,1:T(8,128)(2,1)} %copy.54, bf16[9,16,256,1]{2,1,0,3:T(8,128)(2,1)S(1)} %reshape.865), kind=kOutput, calls=%fused_computation.20 | convolution fusion | flops 377487360 | bytes 5644288 | tf_op jit(solution)/shard_map/dot_general | solution.py:104
  223.3 11.7 %all-to-all-done.1 = f32[256,1,144]{2,1,0:T(1,128)S(1)} async-done(((f32[256,1,144]{2,1,0:T(1,128)}), f32[256,1,144]{2,1,0:T(1,128)S(1)}, u32[]{:S(2)}, u32[]{:S(2)}) %all-to-all-start.1) | async-done | bytes 147488 | tf_op jit(solution)/shard_map/all_to_all | solution.py:138
  236.2 1.1 copy.86
  237.7 1.1 copy.87
  (143 shorter events, 38.4 us)
Async XLA Ops:
  7.2 52.7 %all-gather.4.cloned.1.call-start = ((), (), s32[]{:S(2)}) async-start(), calls=%async_computation.2 | async-start | bytes 2785280 | tf_op jit(solution)/shard_map/all_gather | solution.py:103
  8.2 26.5 %copy-start.3 = (bf16[32,9,8,8]{0,3,2,1:T(8,128)(2,1)S(1)}, bf16[32,9,8,8]{0,3,2,1:T(8,128)(2,1)}, u32[]{:S(2)}) copy-start(bf16[32,9,8,8]{0,3,2,1:T(8,128)(2,1)} %param.8) | copy-start | bytes 110596
  8.2 5.8 %collective-permute-start = (bf16[16,1,512]{2,0,1:T(8,128)(2,1)S(1)}, bf16[16,1,512]{2,0,1:T(8,128)(2,1)S(1)}, u32[]{:S(2)}, u32[]{:S(2)}) collective-permute-start(bf16[16,1,512]{2,0,1:T(8,128)(2,1)S(1)} %get-tuple-element.27), channel_id=1, source_target_pairs={{0,1},{1,2},{2,3},{3,4},{4,5},{5,6},{6,7},{7,8},{8,9},{9,10},{10,1... | collective-permute-start | bytes 49160 | tf_op jit(solution)/shard_map/ppermute | solution.py:21
  12.7 4.7 %collective-permute-start.1 = (bf16[16,1,512]{2,0,1:T(8,128)(2,1)S(1)}, bf16[16,1,512]{2,0,1:T(8,128)(2,1)S(1)}, u32[]{:S(2)}, u32[]{:S(2)}) collective-permute-start(bf16[16,1,512]{2,0,1:T(8,128)(2,1)S(1)} %get-tuple-element.28), channel_id=1, source_target_pairs={{1,0},{2,1},{3,2},{4,3},{5,4},{6,5},{7,6},{8,7},{9,8},{10,9},{11,1... | collective-permute-start | bytes 49160 | tf_op jit(solution)/shard_map/ppermute | solution.py:22
  18.1 81.5 %all-gather.8.cloned.1.call-start = ((), (), s32[]{:S(2)}) async-start(), calls=%async_computation.4 | async-start | bytes 2785280 | tf_op jit(solution)/shard_map/all_gather | solution.py:162
  19.1 4.9 %collective-permute-start.4 = (bf16[16,1,512]{2,0,1:T(8,128)(2,1)S(1)}, bf16[16,1,512]{2,0,1:T(8,128)(2,1)S(1)}, u32[]{:S(2)}, u32[]{:S(2)}) collective-permute-start(bf16[16,1,512]{2,0,1:T(8,128)(2,1)S(1)} %get-tuple-element.29), channel_id=1, source_target_pairs={{0,1},{1,2},{2,3},{3,4},{4,5},{5,6},{6,7},{7,8},{8,9},{9,10},{10,1... | collective-permute-start | bytes 49160 | tf_op jit(solution)/shard_map/ppermute | solution.py:21
  22.6 5.9 %collective-permute-start.5 = (bf16[16,1,512]{2,0,1:T(8,128)(2,1)S(1)}, bf16[16,1,512]{2,0,1:T(8,128)(2,1)S(1)}, u32[]{:S(2)}, u32[]{:S(2)}) collective-permute-start(bf16[16,1,512]{2,0,1:T(8,128)(2,1)S(1)} %get-tuple-element.30), channel_id=1, source_target_pairs={{1,0},{2,1},{3,2},{4,3},{5,4},{6,5},{7,6},{8,7},{9,8},{10,9},{11,1... | collective-permute-start | bytes 49160 | tf_op jit(solution)/shard_map/ppermute | solution.py:22
  29.2 126.8 %all-gather.6.cloned.1.call-start = ((), (), s32[]{:S(2)}) async-start(), calls=%async_computation.3 | async-start | bytes 2785280 | tf_op jit(solution)/shard_map/all_gather | solution.py:103
  32.7 4.8 %copy-start.12 = (s32[8,512]{1,0:T(8,128)S(1)}, s32[8,512]{1,0:T(8,128)}, u32[]{:S(2)}) copy-start(s32[8,512]{1,0:T(8,128)} %param.9) | copy-start | bytes 49156
  108.5 18.1 %copy-start.2 = (bf16[256,10,512]{2,0,1:T(8,128)(2,1)S(1)}, bf16[256,10,512]{2,0,1:T(8,128)(2,1)}, u32[]{:S(2)}) copy-start(bf16[256,10,512]{2,0,1:T(8,128)(2,1)} %all-gather.4.cloned.1.call-done) | copy-start | bytes 7864324
  108.5 4.6 %collective-permute-start.2 = (bf16[16,1,512]{2,0,1:T(8,128)(2,1)S(1)}, bf16[16,1,512]{2,0,1:T(8,128)(2,1)S(1)}, u32[]{:S(2)}, u32[]{:S(2)}) collective-permute-start(bf16[16,1,512]{2,0,1:T(8,128)(2,1)S(1)} %get-tuple-element.25), channel_id=1, source_target_pairs={{0,1},{1,2},{2,3},{3,4},{4,5},{5,6},{6,7},{7,8},{8,9},{9,10},{10,1... | collective-permute-start | bytes 49160 | tf_op jit(solution)/shard_map/ppermute | solution.py:21
  111.8 4.5 %collective-permute-start.3 = (bf16[16,1,512]{2,0,1:T(8,128)(2,1)S(1)}, bf16[16,1,512]{2,0,1:T(8,128)(2,1)S(1)}, u32[]{:S(2)}, u32[]{:S(2)}) collective-permute-start(bf16[16,1,512]{2,0,1:T(8,128)(2,1)S(1)} %get-tuple-element.26), channel_id=1, source_target_pairs={{1,0},{2,1},{3,2},{4,3},{5,4},{6,5},{7,6},{8,7},{9,8},{10,9},{11,1... | collective-permute-start | bytes 49160 | tf_op jit(solution)/shard_map/ppermute | solution.py:22
  117.9 7.7 %collective-permute-start.6 = (bf16[16,1,512]{2,0,1:T(8,128)(2,1)S(1)}, bf16[16,1,512]{2,0,1:T(8,128)(2,1)S(1)}, u32[]{:S(2)}, u32[]{:S(2)}) collective-permute-start(bf16[16,1,512]{2,0,1:T(8,128)(2,1)S(1)} %get-tuple-element.23), channel_id=1, source_target_pairs={{0,1},{1,2},{2,3},{3,4},{4,5},{5,6},{6,7},{7,8},{8,9},{9,10},{10,1... | collective-permute-start | bytes 49160 | tf_op jit(solution)/shard_map/ppermute | solution.py:21
  121.1 5.3 %collective-permute-start.7 = (bf16[16,1,512]{2,0,1:T(8,128)(2,1)S(1)}, bf16[16,1,512]{2,0,1:T(8,128)(2,1)S(1)}, u32[]{:S(2)}, u32[]{:S(2)}) collective-permute-start(bf16[16,1,512]{2,0,1:T(8,128)(2,1)S(1)} %get-tuple-element.24), channel_id=1, source_target_pairs={{1,0},{2,1},{3,2},{4,3},{5,4},{6,5},{7,6},{8,7},{9,8},{10,9},{11,1... | collective-permute-start | bytes 49160 | tf_op jit(solution)/shard_map/ppermute | solution.py:22
  126.6 1.9 copy-start.10
  136.4 2.3 copy-start.9
  136.7 2.0 copy-start.11
  142.3 13.7 %copy-start.1 = (bf16[16,10,512]{2,0,1:T(8,128)(2,1)S(1)}, bf16[16,10,512]{2,0,1:T(8,128)(2,1)}, u32[]{:S(2)}) copy-start(bf16[16,10,512]{2,0,1:T(8,128)(2,1)} %pad_maximum_fusion.2) | copy-start | bytes 491524
  156.0 3.3 %copy-start = (bf16[256,10,512]{2,0,1:T(8,128)(2,1)S(1)}, bf16[256,10,512]{2,0,1:T(8,128)(2,1)}, u32[]{:S(2)}) copy-start(bf16[256,10,512]{2,0,1:T(8,128)(2,1)} %all-gather.6.cloned.1.call-done) | copy-start | bytes 7864324
  160.3 3.2 %copy-start.7 = (bf16[2,8,8,512]{3,2,1,0:T(8,128)(2,1)S(1)}, bf16[2,8,8,512]{3,2,1,0:T(8,128)(2,1)}, u32[]{:S(2)}) copy-start(bf16[2,8,8,512]{3,2,1,0:T(8,128)(2,1)} %param.11) | copy-start | bytes 393220
  169.8 1.6 copy-start.5
  170.6 9.4 %copy-start.13 = (s32[64]{0:T(128)S(1)}, s32[64]{0:T(128)}, u32[]{:S(2)}) copy-start(s32[64]{0:T(128)} %fusion.134) | copy-start | bytes 772
  177.3 0.8 copy-start.6
  180.7 3.1 %copy-start.8 = (f32[128,144]{1,0:T(8,128)S(1)}, f32[128,144]{1,0:T(8,128)}, u32[]{:S(2)}) copy-start(f32[128,144]{1,0:T(8,128)} %concatenate.40) | copy-start | bytes 221188
  180.7 15.8 %copy-start.4 = (bf16[32,9,8,8]{0,3,2,1:T(8,128)(2,1)S(1)}, bf16[32,9,8,8]{0,3,2,1:T(8,128)(2,1)}, u32[]{:S(2)}) copy-start(bf16[32,9,8,8]{0,3,2,1:T(8,128)(2,1)} %param.8) | copy-start | bytes 110596
  184.8 27.3 %all-to-all-start = ((f32[256,1,144]{2,1,0:T(1,128)}), f32[256,1,144]{2,1,0:T(1,128)S(1)}, u32[]{:S(2)}, u32[]{:S(2)}) async-start(f32[256,1,144]{2,1,0:T(1,128)} %copy.84), calls=%async_computation | async-start | bytes 524288 | tf_op jit(solution)/shard_map/all_to_all | solution.py:136
  213.3 21.7 %all-to-all-start.1 = ((f32[256,1,144]{2,1,0:T(1,128)}), f32[256,1,144]{2,1,0:T(1,128)S(1)}, u32[]{:S(2)}, u32[]{:S(2)}) async-start(f32[256,1,144]{2,1,0:T(1,128)} %broadcast_in_dim.2), calls=%async_computation.1 | async-start | bytes 524288 | tf_op jit(solution)/shard_map/all_to_all | solution.py:138
Sparse Core Ops, SparseCore 0:
  18.2 41.6 all-gather.3
  62.3 37.2 all-gather.7
  117.1 38.8 all-gather.5

commit v2 on v1

v2 whole, which is shorter than its diff:
```python
import math

import jax
import jax.numpy as jnp
from jax import lax
from jax.sharding import PartitionSpec as P

G = 32
TAPS = ((0, 0), (0, 1), (0, 2), (1, 0), (1, 1), (1, 2), (2, 0), (2, 1), (2, 2))


def relative(row_ids, col_ids, sector):
    halfway = G // 2
    row_rot = row_ids % halfway
    row_ref = row_ids // halfway
    col_rot = col_ids % halfway
    col_ref = col_ids // halfway
    sec_rot = sector % halfway
    sec_ref = sector // halfway
    moved_rot = (sec_rot + (1 - 2 * sec_ref) * col_rot) % halfway
    moved_ref = (sec_ref + col_ref) % 2
    inverse_rot = jnp.where(row_ref == 0, (halfway - row_rot) % halfway, row_rot)
    result_rot = (inverse_rot + (1 - 2 * row_ref) * moved_rot) % halfway
    result_ref = (row_ref + moved_ref) % 2
    return result_ref * halfway + result_rot


def relation_of(sector):
    ids = jnp.arange(G, dtype=jnp.int32)
    return relative(ids[:, None], ids[None, :], sector).reshape(-1)


def picked_of(kernel, relation):
    taps, channels = kernel.shape[1], kernel.shape[2]
    picked = jnp.take(kernel, relation, axis=0)
    return picked.reshape(G, G, taps, channels, channels)


def forward_matrix(picked):
    width = G * picked.shape[3]
    return picked.transpose(0, 3, 2, 1, 4).reshape(width, -1)


def backward_matrix(picked):
    width = G * picked.shape[3]
    return picked.transpose(1, 4, 2, 0, 3).reshape(width, -1)


def fold(flat_grad, relation, channels):
    taps = len(TAPS)
    arranged = flat_grad.reshape(G, channels, taps, G, channels)
    arranged = arranged.transpose(0, 3, 2, 1, 4).reshape(G * G, -1)
    onehot = (relation[:, None] == jnp.arange(G, dtype=jnp.int32)[None, :]).astype(jnp.float32)
    folded = jnp.dot(
        onehot.T, arranged, precision=lax.Precision.HIGHEST, preferred_element_type=jnp.float32
    )
    return folded.reshape(G, taps, channels, channels)


def windows(grid, height, extent, start=0):
    pieces = [
        grid[:, start + a : start + a + height, start + b : start + b + extent].reshape(grid.shape[0], -1)
        for a, b in TAPS
    ]
    return jnp.concatenate(pieces, axis=0)


def row_halo(block, width):
    count = lax.axis_size("strip")
    up = [(i, i + 1) for i in range(count - 1)]
    down = [(j, i) for i, j in up]
    length = block.shape[1]
    before = lax.ppermute(block[:, length - width :], "strip", up)
    after = lax.ppermute(block[:, :width], "strip", down)
    return jnp.concatenate([before, block, after], axis=1)


def all_sum(flat, axes):
    count = lax.axis_size(axes)
    parts = lax.all_to_all(flat.reshape(count, -1), axes, 0, 0, tiled=True).sum(0)
    spread = jnp.broadcast_to(parts[None], (count,) + parts.shape)
    return lax.all_to_all(spread, axes, 0, 0, tiled=True).reshape(-1)


def shards(inflow_field, kernel_one, kernel_two, turbine_mask, wind_sector, wake_cotangent):
    groups, channels, height, extent = inflow_field.shape
    local_width = groups * channels
    blocks = lax.axis_size("orient")
    span = extent // blocks
    scale_factor = 1.0 / math.sqrt(G * height * lax.axis_size("strip") * extent)
    sector = wind_sector[0]
    rel_one = relation_of(sector)
    rel_two = relation_of(jnp.int32(0))
    picked_one = picked_of(kernel_one, rel_one)
    picked_two = picked_of(kernel_two, rel_two)
    w_one = forward_matrix(picked_one)
    w_two = forward_matrix(picked_two)
    wt_two = backward_matrix(picked_two)

    open_cells = (1 - turbine_mask).astype(jnp.bfloat16)[None]
    stacked = jnp.concatenate(
        [
            inflow_field.reshape(local_width, height, extent),
            wake_cotangent.reshape(local_width, height, extent),
            open_cells,
        ],
        axis=0,
    )
    widened = row_halo(stacked, 2)
    widened = jnp.pad(widened, ((0, 0), (0, 0), (2, 2)))
    mine = lax.axis_index("orient")
    open_here = lax.dynamic_slice_in_dim(widened[2 * local_width :], mine * span, span + 4, axis=2)
    open_here = open_here[0].astype(jnp.float32)
    sending = jnp.stack(
        [widened[: 2 * local_width, :, j * span : j * span + span + 4] for j in range(blocks)], 0
    )
    arrived = lax.all_to_all(sending, "orient", 0, 0, tiled=True)
    full_width = blocks * local_width
    grid_rows, grid_cols = height + 4, span + 4
    source = arrived[:, :local_width].reshape(full_width, grid_rows, grid_cols)
    cotangent = arrived[:, local_width:].reshape(full_width, grid_rows, grid_cols)

    x_cols = windows(source, height + 2, span + 2)
    first_pre = jnp.dot(w_one, x_cols, preferred_element_type=jnp.float32)
    first_pre = first_pre.reshape(full_width, height + 2, span + 2)
    sigmoid_one = jax.nn.sigmoid(first_pre)
    hidden = (first_pre * sigmoid_one * open_here[None, 1:-1, 1:-1]).astype(jnp.bfloat16)

    h_cols = windows(hidden, height, span)
    second_pre = jnp.dot(w_two, h_cols, preferred_element_type=jnp.float32)
    wake = second_pre.astype(jnp.bfloat16).reshape(blocks, local_width, height, span)
    back = lax.all_to_all(wake, "orient", 0, 0, tiled=True)
    wake_out = back.transpose(1, 2, 0, 3).reshape(groups, channels, height, extent)

    cot_rim = cotangent[:, 1:-1, 1:-1]
    cot_mid = cotangent[:, 2:-2, 2:-2].reshape(full_width, -1)
    c_cols = jnp.concatenate(
        [
            cot_rim[:, 2 - a : 2 - a + height, 2 - b : 2 - b + span].reshape(full_width, -1)
            for a, b in TAPS
        ],
        axis=0,
    )
    back_grad = jnp.dot(wt_two, c_cols, preferred_element_type=jnp.float32)
    pre_mid = first_pre[:, 1:-1, 1:-1].reshape(full_width, -1)
    sig_mid = sigmoid_one[:, 1:-1, 1:-1].reshape(full_width, -1)
    open_mid = open_here[2:-2, 2:-2].reshape(1, -1)
    first_grad = (back_grad * open_mid * sig_mid * (1.0 + pre_mid * (1.0 - sig_mid))).astype(
        jnp.bfloat16
    )
    grad_two = lax.dot_general(
        cot_mid, h_cols, (((1,), (1,)), ((), ())), preferred_element_type=jnp.float32
    )
    x_mid = x_cols.reshape(-1, height + 2, span + 2)[:, 1:-1, 1:-1].reshape(x_cols.shape[0], -1)
    grad_one = lax.dot_general(
        first_grad, x_mid, (((1,), (1,)), ((), ())), preferred_element_type=jnp.float32
    )
    share_one = fold(grad_one, rel_one, channels) * scale_factor
    share_two = fold(grad_two, rel_two, channels) * scale_factor
    flat = jnp.concatenate([share_one.reshape(-1), share_two.reshape(-1)])
    flat = all_sum(flat, ("orient", "strip"))
    summed_one, summed_two = jnp.split(flat, 2)
    return (wake_out, summed_one.reshape(share_one.shape), summed_two.reshape(share_two.shape))


def solution(mesh):
    return jax.shard_map(
        shards,
        mesh=mesh,
        in_specs=(
            P("orient", None, "strip", None),
            P(),
            P(),
            P("strip", None),
            P(),
            P("orient", None, "strip", None),
        ),
        out_specs=(P("orient", None, "strip", None), P(), P()),
        check_vma=False,
    )
```

time: 247 us -> 546 us (2.21); the launches traced: 245 us -> 538 us
  local copies, waits for them, and re-layouts: 57.2 us -> 420 us
  waiting for transfers between devices: 97.5 us -> 19.7 us
  other arithmetic: 6.11 us -> 31.3 us
  between operations: 15.1 us -> 2.28 us
  matrix products: 31.7 us -> 19.3 us
  starting transfers between devices: 37.7 us -> 45.7 us
    reshape x4 -> x33, local copies, waits for them, and re-layouts: 1.64 us -> 277 us  [the longest x3 171 us: picked_of(): return picked.reshape(G, G, taps, channels, channels)]
    all_gather x3 -> x0, waiting for transfers between devices: 66.2 us -> none  [the longest x2 33.7 us: layer_forward(): gathered = lax.all_gather(widened, 'orient', axis=0, tiled=True)]
    slice x4 -> x32, local copies, waits for them, and re-layouts: 0.02 us -> 36 us  [the longest x11 15.2 us: shards(): cot_rim[:, 2 - a:2 - a + height, 2 - b:2 - b + span].reshape(full_width, -1)]
    select_n x0 -> x4, other arithmetic: none -> 29.9 us  [the longest x2 29.9 us: picked_of(): picked = jnp.take(kernel, relation, axis=0)]
    unnamed x48 -> x92, local copies, waits for them, and re-layouts: 11.5 us -> 39.2 us
    gather x0 -> x2, local copies, waits for them, and re-layouts: none -> 27.1 us  [picked_of(): picked = jnp.take(kernel, relation, axis=0)]
    transpose x2 -> x3, local copies, waits for them, and re-layouts: 1.98 us -> 22.7 us  [the longest x2 22.3 us: fold(): arranged = arranged.transpose(0, 3, 2, 1, 4).reshape(G * G, -1)]
    ppermute x8 -> x2, starting transfers between devices: 19.9 us -> 5.66 us  [the longest x1 4.36 us: row_halo(): before = lax.ppermute(block[:, length - width:], 'strip', up)]
  transfers between devices with their start and end apart: 13 -> 6, of which waited for: 9 -> 2; matrix products, arithmetic and copies ran while one was open for 20% -> 59% of each run, Pallas kernels for 0% -> 0%
where the time goes in v2:
time: 546 us; the launch traced here: 538 us
  local copies, waits for them, and re-layouts  420 us (77%)
  starting transfers between devices  45.7 us (8%)
  other arithmetic  31.3 us (6%)
  waiting for transfers between devices  19.7 us (4%)
  matrix products  19.3 us (4%)
    reshape x3, local copies, waits for them, and re-layouts, picked_of(): return picked.reshape(G, G, taps, channels, channels)  171 us
    reshape x2, local copies, waits for them, and re-layouts, forward_matrix(): return picked.transpose(0, 3, 2, 1, 4).reshape(width, -1)  54.3 us
    unnamed x92, local copies, waits for them, and re-layouts  39.2 us
    select_n x2, other arithmetic, picked_of(): picked = jnp.take(kernel, relation, axis=0)  29.9 us
    reshape x1, local copies, waits for them, and re-layouts, backward_matrix(): return picked.transpose(1, 4, 2, 0, 3).reshape(width, -1)  28 us
    gather x2, local copies, waits for them, and re-layouts, picked_of(): picked = jnp.take(kernel, relation, axis=0)  27.1 us
    transpose x2, local copies, waits for them, and re-layouts, fold(): arranged = arranged.transpose(0, 3, 2, 1, 4).reshape(G * G, -1)  22.3 us
    all_to_all x1, starting transfers between devices, all_sum(): lax.all_to_all(flat.reshape(count, -1), axes, 0, 0, tiled=True).sum(0)  16.1 us
  transfers between devices with their start and end apart: 6, of which 2 were waited for; matrix products, arithmetic and copies ran while one was open for 59% of the time, Pallas kernels for 0%

profile of v2, /device:TPU:1, one launch (start us, length us, event | category | flops | bytes accessed | tf_op | source)
XLA Modules:
  0.0 538.2 jit_solution(4250071106643285436)
XLA Ops:
  2.5 4.4 collective-permute-start
  9.2 1.9 copy.173
  11.3 13.5 %gather_fusion.1 = bf16[1024,9,8,8]{1,3,2,0:T(8,128)(2,1)} fusion(bf16[32,9,8,8]{1,3,2,0:T(8,128)(2,1)S(1)} %copy.173, s32[1024]{0:T(1024)S(1)} %fusion.42), kind=kCustom, calls=%fused_computation.1.clone | custom fusion | bytes 2363392 | tf_op jit(solution)/shard_map/jit(_take)/gather | solution.py:35
  24.8 15.0 %broadcast_select_fusion = bf16[1024,9,8,8]{1,3,2,0:T(8,128)(2,1)} fusion(bf16[1024,9,8,8]{1,3,2,0:T(8,128)(2,1)} %gather_fusion.1, pred[1024]{0:T(1024)(128)(4,1)S(1)} %get-tuple-element.18), kind=kLoop, calls=%fused_computation.2 | loop fusion | flops 589824 | bytes 2360320 | tf_op jit(solution)/shard_map/jit(_take)/select_n | solution.py:35
  40.8 13.6 %gather_fusion = bf16[1024,9,8,8]{1,3,2,0:T(8,128)(2,1)} fusion(bf16[32,9,8,8]{1,3,2,0:T(8,128)(2,1)S(1)} %copy.171, s32[1024]{0:T(1024)S(1)} %fusion.41), kind=kCustom, calls=%fused_computation.clone | custom fusion | bytes 2363392 | tf_op jit(solution)/shard_map/jit(_take)/gather | solution.py:35
  56.3 4.7 reshape.628
  61.0 6.7 %all-to-all-start = ((bf16[16,2,6912]{2,1,0:T(2,128)(2,1)}), bf16[16,2,6912]{2,1,0:T(2,128)(2,1)S(1)}, u32[]{:S(2)}, u32[]{:S(2)}) async-start(bf16[16,2,6912]{2,1,0:T(2,128)(2,1)} %reshape.628), calls=%async_computation | async-start | bytes 884736 | tf_op jit(solution)/shard_map/all_to_all | solution.py:117
  67.7 14.9 %broadcast_select_fusion.1 = bf16[1024,9,8,8]{1,3,2,0:T(8,128)(2,1)} fusion(bf16[1024,9,8,8]{1,3,2,0:T(8,128)(2,1)} %gather_fusion, pred[1024]{0:T(1024)(128)(4,1)S(1)} %get-tuple-element.20), kind=kLoop, calls=%fused_computation.3 | loop fusion | flops 589824 | bytes 2360320 | tf_op jit(solution)/shard_map/jit(_take)/select_n | solution.py:35
  82.7 56.6 %copy.174 = bf16[32,32,9,8,8]{4,1,2,3,0:T(8,128)(2,1)} copy(bf16[32,32,9,8,8]{2,4,3,1,0:T(8,128)(2,1)} %bitcast.198) | data formatting | bytes 2359296 | tf_op jit(solution)/shard_map/reshape | solution.py:36
  139.2 27.5 %reshape.617 = bf16[256,2304,1]{1,0,2:T(8,128)(2,1)} reshape(bf16[32,8,9,32,8]{4,3,2,1,0:T(8,128)(2,1)} %bitcast.195) | data formatting | bytes 2359296 | tf_op jit(solution)/shard_map/reshape | solution.py:41
  166.7 57.6 %copy.198 = bf16[32,32,9,8,8]{3,0,2,4,1:T(8,128)(2,1)} copy(bf16[32,32,9,8,8]{2,4,3,1,0:T(8,128)(2,1)} %bitcast.193) | data formatting | bytes 2359296 | tf_op jit(solution)/shard_map/reshape | solution.py:36
  224.4 28.0 %reshape.577 = bf16[256,2304]{1,0:T(8,128)(2,1)} reshape(bf16[32,8,9,32,8]{4,3,2,1,0:T(8,128)(2,1)} %bitcast.197) | data formatting | bytes 2359296 | tf_op jit(solution)/shard_map/reshape | solution.py:46
  253.4 4.5 reshape.629
  258.4 3.3 fusion.53
  261.7 1.4 copy.179
  264.7 2.9 fusion.52
  271.6 1.9 copy.201
  273.5 1.9 copy.202
  275.4 1.9 copy.203
  280.6 1.4 copy.180
  282.8 1.4 copy.181
  286.0 1.4 copy.183
  297.0 1.7 slice.292
  298.6 5.1 copy.221
  303.7 6.0 %dot_general.47 = bf16[9,32,8,256]{3,2,1,0:T(8,128)(2,1)S(1)} reshape(bf16[2304,8,32]{2,1,0:T(8,128)(2,1)} %copy.221) | data formatting | bytes 2359296 | tf_op jit(solution)/shard_map/dot_general | solution.py:155
  316.1 3.4 dot_general.42
  319.6 3.0 add_divide_fusion
  324.0 1.7 constant_dynamic-update-slice_fusion.41
  325.7 1.6 constant_dynamic-update-slice_fusion.40
  327.2 1.6 constant_dynamic-update-slice_fusion.39
  329.5 1.6 constant_dynamic-update-slice_fusion.37
  331.1 1.6 constant_dynamic-update-slice_fusion.36
  334.1 7.3 %convolution_bitcast_fusion.1 = f32[32,32,9,8,8]{1,3,4,2,0:T(8,128)} fusion(bf16[9,32,8,256]{3,2,1,0:T(8,128)(2,1)S(1)} %dot_general.47, f32[256,256]{1,0:T(8,128)S(1)} %copy.209, bf16[256,2304]{1,0:T(8,128)(2,1)S(1)} %copy-done, bf16[2304,256]{0,1:T(8,128)(2,1)} %constant_dynamic-update-slice_fusion.34, f32[256,256]{1,0:T(8,128)S(1)} %copy.211, ...), kind=kOutput, calls=%fused_computation.9 | convolution fusion | flops 604438528 | bytes 6423552 | tf_op jit(solution)/shard_map/dot_general | solution.py:155
  341.4 12.8 %copy.223 = f32[32,32,9,8,8]{1,0,4,3,2:T(8,128)} copy(f32[32,32,9,8,8]{1,3,4,2,0:T(8,128)} %convolution_bitcast_fusion.1) | data formatting | bytes 4718592 | tf_op jit(solution)/shard_map/transpose | solution.py:52
  354.2 7.4 %reshape.590 = f32[1024,576]{0,1:T(8,128)S(1)} reshape(f32[32,32,9,8,8]{1,0,4,3,2:T(8,128)} %copy.223) | data formatting | bytes 4718592 | tf_op jit(solution)/shard_map/reshape | solution.py:52
  361.6 3.2 fusion.4
  368.0 1.4 convolution_bitcast_fusion
  369.4 9.5 %copy.228 = f32[32,32,9,8,8]{1,0,4,3,2:T(8,128)} copy(f32[32,32,9,8,8]{1,3,4,2,0:T(8,128)S(1)} %convolution_bitcast_fusion) | data formatting | bytes 4718592 | tf_op jit(solution)/shard_map/transpose | solution.py:52
  378.9 7.2 %reshape.591 = f32[1024,576]{0,1:T(8,128)S(1)} reshape(f32[32,32,9,8,8]{1,0,4,3,2:T(8,128)} %copy.228) | data formatting | bytes 4718592 | tf_op jit(solution)/shard_map/reshape | solution.py:52
  386.1 4.0 fusion.7
  390.1 1.5 copy.230
  393.0 16.1 %all-to-all-start.2 = ((f32[256,1,144]{2,1,0:T(1,128)}), f32[256,1,144]{2,1,0:T(1,128)S(1)}, u32[]{:S(2)}, u32[]{:S(2)}) async-start(f32[256,1,144]{2,1,0:T(1,128)} %copy.231), calls=%async_computation.2 | async-start | bytes 524288 | tf_op jit(solution)/shard_map/all_to_all | solution.py:80
  409.1 56.6 %copy.172 = bf16[32,32,9,8,8]{4,1,2,3,0:T(8,128)(2,1)} copy(bf16[32,32,9,8,8]{2,4,3,1,0:T(8,128)(2,1)} %bitcast.194) | data formatting | bytes 2359296 | tf_op jit(solution)/shard_map/reshape | solution.py:36
  465.7 26.8 %reshape.551 = bf16[256,2304]{1,0:T(8,128)(2,1)S(1)} reshape(bf16[32,8,9,32,8]{4,3,2,1,0:T(8,128)(2,1)} %bitcast.196) | data formatting | bytes 2359296 | tf_op jit(solution)/shard_map/reshape | solution.py:41
  494.5 5.7 %all-to-all-start.1 = ((bf16[16,2,2048]{2,1,0:T(2,128)(2,1)}), bf16[16,2,2048]{2,1,0:T(2,128)(2,1)S(1)}, u32[]{:S(2)}, u32[]{:S(2)}) async-start(bf16[16,2,2048]{2,1,0:T(2,128)(2,1)} %reshape.630), calls=%async_computation.1 | async-start | bytes 262144 | tf_op jit(solution)/shard_map/all_to_all | solution.py:132
  500.5 5.8 %all-to-all-done.1 = bf16[16,2,2048]{2,1,0:T(2,128)(2,1)S(1)} async-done(((bf16[16,2,2048]{2,1,0:T(2,128)(2,1)}), bf16[16,2,2048]{2,1,0:T(2,128)(2,1)S(1)}, u32[]{:S(2)}, u32[]{:S(2)}) %all-to-all-start.1) | async-done | bytes 131104 | tf_op jit(solution)/shard_map/all_to_all | solution.py:132
  507.2 11.4 %all-to-all-start.3 = ((f32[256,1,144]{2,1,0:T(1,128)}), f32[256,1,144]{2,1,0:T(1,128)S(1)}, u32[]{:S(2)}, u32[]{:S(2)}) async-start(f32[256,1,144]{2,1,0:T(1,128)} %broadcast_in_dim.14), calls=%async_computation.3 | async-start | bytes 524288 | tf_op jit(solution)/shard_map/all_to_all | solution.py:82
  520.3 13.9 %all-to-all-done.3 = f32[256,1,144]{2,1,0:T(1,128)S(1)} async-done(((f32[256,1,144]{2,1,0:T(1,128)}), f32[256,1,144]{2,1,0:T(1,128)S(1)}, u32[]{:S(2)}, u32[]{:S(2)}) %all-to-all-start.3) | async-done | bytes 147488 | tf_op jit(solution)/shard_map/all_to_all | solution.py:82
  (171 shorter events, 51.9 us)
Async XLA Ops:
  2.5 51.9 %collective-permute-start = (bf16[33,2,512]{2,0,1:T(8,128)(2,1)S(1)}, bf16[33,2,512]{2,0,1:T(8,128)(2,1)S(1)}, u32[]{:S(2)}, u32[]{:S(2)}) collective-permute-start(bf16[33,2,512]{2,0,1:T(8,128)(2,1)S(1)} %get-tuple-element.44), channel_id=1, source_target_pairs={{0,1},{1,2},{2,3},{3,4},{4,5},{5,6},{6,7},{7,8},{8,9},{9,10},{10,1... | collective-permute-start | bytes 202760 | tf_op jit(solution)/shard_map/ppermute | solution.py:73
  6.8 47.6 %collective-permute-start.1 = (bf16[33,2,512]{2,0,1:T(8,128)(2,1)S(1)}, bf16[33,2,512]{2,0,1:T(8,128)(2,1)S(1)}, u32[]{:S(2)}, u32[]{:S(2)}) collective-permute-start(bf16[33,2,512]{2,0,1:T(8,128)(2,1)S(1)} %get-tuple-element.45), channel_id=1, source_target_pairs={{1,0},{2,1},{3,2},{4,3},{5,4},{6,5},{7,6},{8,7},{9,8},{10,9},{11,1... | collective-permute-start | bytes 202760 | tf_op jit(solution)/shard_map/ppermute | solution.py:74
  24.8 15.0 %copy-start.16 = (bf16[32,9,8,8]{0,3,2,1:T(8,128)(2,1)S(1)}, bf16[32,9,8,8]{0,3,2,1:T(8,128)(2,1)}, u32[]{:S(2)}) copy-start(bf16[32,9,8,8]{0,3,2,1:T(8,128)(2,1)} %param.10) | copy-start | bytes 110596
  61.0 192.4 %all-to-all-start = ((bf16[16,2,6912]{2,1,0:T(2,128)(2,1)}), bf16[16,2,6912]{2,1,0:T(2,128)(2,1)S(1)}, u32[]{:S(2)}, u32[]{:S(2)}) async-start(bf16[16,2,6912]{2,1,0:T(2,128)(2,1)} %reshape.628), calls=%async_computation | async-start | bytes 884736 | tf_op jit(solution)/shard_map/all_to_all | solution.py:117
  269.7 7.6 %copy-start.3 = (bf16[256,8,32]{2,0,1:T(8,128)(2,1)S(1)}, bf16[256,8,32]{2,0,1:T(8,128)(2,1)}, u32[]{:S(2)}) copy-start(bf16[256,8,32]{2,0,1:T(8,128)(2,1)} %get-tuple-element.27) | copy-start | bytes 393220
  280.6 4.3 copy-start.2
  286.0 5.7 %copy-start.1 = (bf16[256,10,34]{2,0,1:T(8,128)(2,1)S(1)}, bf16[256,10,34]{2,0,1:T(8,128)(2,1)}, u32[]{:S(2)}) copy-start(bf16[256,10,34]{2,0,1:T(8,128)(2,1)} %get-tuple-element.35) | copy-start | bytes 522244
  303.7 6.0 %copy-start.6 = (bf16[256,340]{0,1:T(8,128)(2,1)S(1)}, bf16[256,340]{0,1:T(8,128)(2,1)}, u32[]{:S(2)}) copy-start(bf16[256,340]{0,1:T(8,128)(2,1)} %reshape.557) | copy-start | bytes 522244
  303.7 8.8 %copy-start.7 = (bf16[256,340]{0,1:T(8,128)(2,1)S(1)}, bf16[256,340]{0,1:T(8,128)(2,1)}, u32[]{:S(2)}) copy-start(bf16[256,340]{0,1:T(8,128)(2,1)} %reshape.561) | copy-start | bytes 522244
  309.7 3.6 copy-start.8
  309.7 4.3 copy-start.9
  309.7 4.9 copy-start.10
  309.7 5.7 %copy-start.11 = (bf16[256,340]{0,1:T(8,128)(2,1)S(1)}, bf16[256,340]{0,1:T(8,128)(2,1)}, u32[]{:S(2)}) copy-start(bf16[256,340]{0,1:T(8,128)(2,1)} %reshape.565) | copy-start | bytes 522244
  316.1 3.4 copy-start.5
  316.1 3.4 copy-start.17
  322.6 6.3 %copy-start.12 = (bf16[256,8,32]{0,2,1:T(8,128)(2,1)S(1)}, bf16[256,8,32]{0,2,1:T(8,128)(2,1)}, u32[]{:S(2)}) copy-start(bf16[256,8,32]{0,2,1:T(8,128)(2,1)} %copy.204) | copy-start | bytes 393220
  322.7 11.4 %copy-start = (bf16[256,2304]{1,0:T(8,128)(2,1)S(1)}, bf16[256,2304]{1,0:T(8,128)(2,1)}, u32[]{:S(2)}) copy-start(bf16[256,2304]{1,0:T(8,128)(2,1)} %reshape.577) | copy-start | bytes 3538948
  324.0 8.7 %copy-start.13 = (bf16[256,8,32]{0,2,1:T(8,128)(2,1)S(1)}, bf16[256,8,32]{0,2,1:T(8,128)(2,1)}, u32[]{:S(2)}) copy-start(bf16[256,8,32]{0,2,1:T(8,128)(2,1)} %copy.207) | copy-start | bytes 393220
  324.0 9.4 %copy-start.14 = (bf16[256,8,32]{0,2,1:T(8,128)(2,1)S(1)}, bf16[256,8,32]{0,2,1:T(8,128)(2,1)}, u32[]{:S(2)}) copy-start(bf16[256,8,32]{0,2,1:T(8,128)(2,1)} %copy.208) | copy-start | bytes 393220
  366.5 1.0 copy-start.4
  390.1 1.9 copy-start.15
  393.0 101.5 %all-to-all-start.2 = ((f32[256,1,144]{2,1,0:T(1,128)}), f32[256,1,144]{2,1,0:T(1,128)S(1)}, u32[]{:S(2)}, u32[]{:S(2)}) async-start(f32[256,1,144]{2,1,0:T(1,128)} %copy.231), calls=%async_computation.2 | async-start | bytes 524288 | tf_op jit(solution)/shard_map/all_to_all | solution.py:80
  494.5 11.8 %all-to-all-start.1 = ((bf16[16,2,2048]{2,1,0:T(2,128)(2,1)}), bf16[16,2,2048]{2,1,0:T(2,128)(2,1)S(1)}, u32[]{:S(2)}, u32[]{:S(2)}) async-start(bf16[16,2,2048]{2,1,0:T(2,128)(2,1)} %reshape.630), calls=%async_computation.1 | async-start | bytes 262144 | tf_op jit(solution)/shard_map/all_to_all | solution.py:132
  507.2 27.0 %all-to-all-start.3 = ((f32[256,1,144]{2,1,0:T(1,128)}), f32[256,1,144]{2,1,0:T(1,128)S(1)}, u32[]{:S(2)}, u32[]{:S(2)}) async-start(f32[256,1,144]{2,1,0:T(1,128)} %broadcast_in_dim.14), calls=%async_computation.3 | async-start | bytes 524288 | tf_op jit(solution)/shard_map/all_to_all | solution.py:82
